TPU v7x, 128 devices: a whole 4x4x4 slice. The times are simulated.
128 devices in a mesh: seq: 16 (over y_hi, x, core), head: 8 (over z, y_lo).
Axes of the slice: x: 4, y: 4 (y_hi: 2, y_lo: 2; y = y_hi * 2 + y_lo), z: 4, core: 2. Of those that a mesh axis runs over, the one named last changes fastest.
Arguments:
- inputs_x: bfloat16 [4096, 8192], P('seq', 'head'), may hold values from -6 to 6
- inputs_b: bfloat16 [4096, 1024], P('seq', 'head'), may hold values from -0.59765625 to 0.59765625
- inputs_c: bfloat16 [4096, 1024], P('seq', 'head'), may hold values from -6 to 6
- gate_z: bfloat16 [4096, 8192], P('seq', 'head'), may hold values from -6 to 6
- log_decay: float32 [128, 4096], P('head', 'seq'), may hold values from -1 to 0, as said below
- resets: int32 [4096], P('seq'), may hold values from 0 to 1, as said below
- norm_gain: float32 [8192], P('head'), may hold values from 0.1 to 1.9
- out_weight: bfloat16 [4096, 8192], P('seq', 'head'), may hold values from -0.09375 to 0.09375
- out_grad: bfloat16 [4096, 4096], P('seq', 'head'), may hold values from -6 to 6
Outputs:
- layer_out: bfloat16 [4096, 4096], P('seq', 'head')
- grad_x: float32 [4096, 8192], P('seq', 'head')
- grad_b: float32 [4096, 1024], P('seq', 'head')
- grad_c: float32 [4096, 1024], P('seq', 'head')
- grad_z: float32 [4096, 8192], P('seq', 'head')
- grad_decay: float32 [128, 4096], P('head', 'seq')
- grad_weight: float32 [4096, 8192], P('seq', 'head')
Inputs may be any that keep to these rules, and one draw needn't show every extreme that they name: `log_decay`: the decay factor of a token is exp of its entry. `resets`: exactly one entry is 1, the first token of the second rollout, at a position from 512 to 3583.
All inputs are finite; a program needn't handle non-finite values.
Results may differ from a plain program's by a relative error of at most 0.023.
Values may be sent and summed in bfloat16 or wider, within the bound.
No kernel may reach another device: no remote copies, remote signals or barrier semaphores. Data moves between devices by JAX's collectives and lax.ppermute only.
A program may use at most 128 MiB of HBM per device.

v0:
```python
import jax
import jax.numpy as jnp
from jax import lax
from jax.sharding import PartitionSpec as P

P_SIZE = 64
N = 128
G = 8
SPAN = 256
HP = 8192


def from_behind(value, axis, steps):
    count = lax.axis_size(axis)
    leading, last = (max(0, -steps), min(count, count - steps))
    return lax.ppermute(value, axis, [(source, source + steps) for source in range(leading, last)])


def span_scan(inputs_x, inputs_b, inputs_c, log_decay, resets, start_state):
    tokens_here = inputs_x.shape[0]
    heads_here = log_decay.shape[0]
    groups_here = inputs_b.shape[1] // N
    repeat_count = heads_here // groups_here
    blocks = tokens_here // SPAN
    x_blocks = inputs_x.reshape(blocks, SPAN, heads_here, P_SIZE)
    b_blocks = inputs_b.reshape(blocks, SPAN, groups_here, N)
    c_blocks = inputs_c.reshape(blocks, SPAN, groups_here, N)
    d_blocks = log_decay.reshape(heads_here, blocks, SPAN).transpose(1, 0, 2)
    r_blocks = resets.reshape(blocks, SPAN)
    order = jnp.arange(SPAN, dtype=jnp.int32)
    lower = order[None, :] <= order[:, None]

    def advance(state, pieces):
        x_here, b_here, c_here, d_here, r_here = pieces
        cumul = jnp.cumsum(d_here, axis=1)
        counts = jnp.cumsum(r_here)
        same = lower & (counts[:, None] == counts[None, :])
        spread = cumul[:, :, None] - cumul[:, None, :]
        weights = jnp.where(same[None], jnp.exp(jnp.minimum(spread, 0.0)), 0.0)
        scores = jnp.einsum("tgn,sgn->gts", c_here, b_here, precision=lax.Precision.HIGHEST)
        scores = jnp.repeat(scores, repeat_count, axis=0) * weights
        inner = jnp.einsum("hts,shp->thp", scores, x_here, precision=lax.Precision.HIGHEST)
        c_heads = jnp.repeat(c_here, repeat_count, axis=1)
        b_heads = jnp.repeat(b_here, repeat_count, axis=1)
        entry = jnp.exp(cumul) * (counts == 0).astype(jnp.float32)[None, :]
        carried = (
            jnp.einsum("thn,hpn->thp", c_heads, state, precision=lax.Precision.HIGHEST)
            * entry.T[:, :, None]
        )
        tail = jnp.exp(cumul[:, -1:] - cumul) * (counts == counts[-1]).astype(jnp.float32)[None, :]
        fresh = jnp.einsum(
            "shp,shn->hpn", x_here * tail.T[:, :, None], b_heads, precision=lax.Precision.HIGHEST
        )
        passing = entry[:, -1]
        return (fresh + passing[:, None, None] * state, inner + carried)

    final, outputs = lax.scan(
        jax.checkpoint(advance), start_state, (x_blocks, b_blocks, c_blocks, d_blocks, r_blocks)
    )
    return (outputs.reshape(tokens_here, heads_here * P_SIZE), final)


def gated_norm(values, gate, gain):
    gated = values * jax.nn.silu(gate)
    rows_here, width = gated.shape
    group_width = HP // G
    grouped = gated.reshape(rows_here, width // group_width, group_width)
    scale = lax.rsqrt(jnp.mean(grouped * grouped, axis=2, keepdims=True) + 1e-05)
    return (grouped * scale).reshape(rows_here, width) * gain[None, :]


def carried_term(inputs_c, log_decay, resets, state):
    heads_here = log_decay.shape[0]
    tokens_here = inputs_c.shape[0]
    groups_here = inputs_c.shape[1] // N
    cumul = jnp.cumsum(log_decay, axis=1)
    counts = jnp.cumsum(resets)
    entry = jnp.exp(cumul) * (counts == 0).astype(jnp.float32)[None, :]
    c_heads = jnp.repeat(
        inputs_c.reshape(tokens_here, groups_here, N), heads_here // groups_here, axis=1
    )
    result = (
        jnp.einsum("thn,hpn->thp", c_heads, state, precision=lax.Precision.HIGHEST)
        * entry.T[:, :, None]
    )
    return result.reshape(tokens_here, heads_here * P_SIZE)


def device_decay(log_decay, resets):
    return jnp.exp(jnp.sum(log_decay, axis=1)) * (jnp.sum(resets) == 0).astype(jnp.float32)


def per_device(
    inputs_x, inputs_b, inputs_c, gate_z, log_decay, resets, norm_gain, out_weight, out_grad
):
    x_float = inputs_x.astype(jnp.float32)
    b_float = inputs_b.astype(jnp.float32)
    c_float = inputs_c.astype(jnp.float32)
    z_float = gate_z.astype(jnp.float32)
    heads_here = log_decay.shape[0]
    zero_state = jnp.zeros((heads_here, P_SIZE, N), jnp.float32)

    def local_scan(x_arg, b_arg, c_arg, decay_arg):
        return span_scan(x_arg, b_arg, c_arg, decay_arg, resets, zero_state)

    (y_zero, s_local), pull_scan = jax.vjp(local_scan, x_float, b_float, c_float, log_decay)

    def whole_decay(decay_arg):
        return device_decay(decay_arg, resets)

    g_local, pull_decay = jax.vjp(whole_decay, log_decay)

    def forward_step(turn, carried):
        return from_behind(
            (g_local[:, None, None] * carried + s_local).astype(jnp.bfloat16), "seq", 1
        ).astype(jnp.float32)

    state_in = lax.fori_loop(0, lax.axis_size("seq") - 1, forward_step, zero_state)

    def finish(y_arg, c_arg, decay_arg, z_arg, state_arg):
        return gated_norm(
            y_arg + carried_term(c_arg, decay_arg, resets, state_arg), z_arg, norm_gain
        )

    normed, pull_finish = jax.vjp(finish, y_zero, c_float, log_decay, z_float, state_in)
    normed_bf = normed.astype(jnp.bfloat16)
    full_weight = lax.all_gather(out_weight, "seq", axis=0, tiled=True)
    partial_value = lax.dot_general(
        normed_bf, full_weight, (((1,), (1,)), ((), ())), preferred_element_type=jnp.float32
    )
    layer_out = lax.psum_scatter(
        partial_value.astype(jnp.bfloat16), "head", scatter_dimension=1, tiled=True
    )
    grad_full = lax.all_gather(out_grad, "head", axis=1, tiled=True)
    grad_y = jnp.dot(grad_full, full_weight, preferred_element_type=jnp.float32)
    grad_weight = lax.psum_scatter(
        lax.dot_general(
            grad_full, normed_bf, (((0,), (0,)), ((), ())), preferred_element_type=jnp.float32
        ).astype(jnp.bfloat16),
        "seq",
        scatter_dimension=0,
        tiled=True,
    ).astype(jnp.float32)
    d_zero, d_c_two, d_decay_two, grad_z, adjoint_in = pull_finish(grad_y)

    def backward_step(turn, carried):
        return from_behind(
            (g_local[:, None, None] * carried + adjoint_in).astype(jnp.bfloat16), "seq", -1
        ).astype(jnp.float32)

    adjoint_out = lax.fori_loop(0, lax.axis_size("seq") - 1, backward_step, zero_state)
    grad_x, grad_b, d_c_one, d_decay_one = pull_scan((d_zero, adjoint_out))
    (d_decay_three,) = pull_decay(jnp.sum(adjoint_out * state_in, axis=(1, 2)))
    return (
        layer_out,
        grad_x,
        grad_b,
        d_c_one + d_c_two,
        grad_z,
        d_decay_one + d_decay_two + d_decay_three,
        grad_weight,
    )


def solution(mesh):
    return jax.shard_map(
        per_device,
        mesh=mesh,
        in_specs=(
            P("seq", "head"),
            P("seq", "head"),
            P("seq", "head"),
            P("seq", "head"),
            P("head", "seq"),
            P("seq"),
            P("head"),
            P("seq", "head"),
            P("seq", "head"),
        ),
        out_specs=(
            P("seq", "head"),
            P("seq", "head"),
            P("seq", "head"),
            P("seq", "head"),
            P("seq", "head"),
            P("head", "seq"),
            P("seq", "head"),
        ),
        check_vma=False,
    )
```

profile of v0, /device:TPU:0, one launch (start us, length us, event | category | flops | bytes accessed | tf_op | source)
XLA Modules:
  0.0 496.0 jit_solution(6926276230985404334)
XLA Ops:
  20.6 136.6 %while.6 = (s32[]{:T(128)}, f32[16,64,128]{2,1,0:T(8,128)S(1)}, f32[16]{0:T(128)S(1)}, f32[16,64,128]{2,1,0:T(8,128)S(1)}, s32[]{:T(128)}, /*index=5*/s32[]{:T(128)}) while((s32[]{:T(128)}, f32[16,64,128]{2,1,0:T(8,128)S(1)}, f32[16]{0:T(128)S(1)}, f32[16,64,128]{2,1,0:T(8,128)S(1)}, s32[]{:T(128)}, /*index=5*/s32[]{:T(128)}) %tuple.72), condition=%wide.region_7.8_spmd.clone, body=%wide.region_6.7_spmd.clone.sunk | while | flops 655363 | bytes 3145911 | solution.py:118
  31.1 6.6 %collective-permute-start = (bf16[16,64,128]{2,1,0:T(8,128)(2,1)S(1)}, bf16[16,64,128]{2,1,0:T(8,128)(2,1)S(1)}, u32[]{:S(2)}, u32[]{:S(2)}) collective-permute-start(bf16[16,64,128]{2,1,0:T(8,128)(2,1)S(1)} %fusion.120), channel_id=1, source_target_pairs={{0,8},{8,16},{16,24},{24,32},{32,40},{40,48},{48,56},{56,64},{64,7... | collective-permute-start | bytes 786440 | tf_op jit(solution)/shard_map/while/body/eval_jaxpr/ppermute | solution.py:16
  39.0 6.6 %collective-permute-start = (bf16[16,64,128]{2,1,0:T(8,128)(2,1)S(1)}, bf16[16,64,128]{2,1,0:T(8,128)(2,1)S(1)}, u32[]{:S(2)}, u32[]{:S(2)}) collective-permute-start(bf16[16,64,128]{2,1,0:T(8,128)(2,1)S(1)} %fusion.120), channel_id=1, source_target_pairs={{0,8},{8,16},{16,24},{24,32},{32,40},{40,48},{48,56},{56,64},{64,7... | collective-permute-start | bytes 786440 | tf_op jit(solution)/shard_map/while/body/eval_jaxpr/ppermute | solution.py:16
  46.9 6.6 %collective-permute-start = (bf16[16,64,128]{2,1,0:T(8,128)(2,1)S(1)}, bf16[16,64,128]{2,1,0:T(8,128)(2,1)S(1)}, u32[]{:S(2)}, u32[]{:S(2)}) collective-permute-start(bf16[16,64,128]{2,1,0:T(8,128)(2,1)S(1)} %fusion.120), channel_id=1, source_target_pairs={{0,8},{8,16},{16,24},{24,32},{32,40},{40,48},{48,56},{56,64},{64,7... | collective-permute-start | bytes 786440 | tf_op jit(solution)/shard_map/while/body/eval_jaxpr/ppermute | solution.py:16
  54.8 6.6 %collective-permute-start = (bf16[16,64,128]{2,1,0:T(8,128)(2,1)S(1)}, bf16[16,64,128]{2,1,0:T(8,128)(2,1)S(1)}, u32[]{:S(2)}, u32[]{:S(2)}) collective-permute-start(bf16[16,64,128]{2,1,0:T(8,128)(2,1)S(1)} %fusion.120), channel_id=1, source_target_pairs={{0,8},{8,16},{16,24},{24,32},{32,40},{40,48},{48,56},{56,64},{64,7... | collective-permute-start | bytes 786440 | tf_op jit(solution)/shard_map/while/body/eval_jaxpr/ppermute | solution.py:16
  62.7 6.6 %collective-permute-start = (bf16[16,64,128]{2,1,0:T(8,128)(2,1)S(1)}, bf16[16,64,128]{2,1,0:T(8,128)(2,1)S(1)}, u32[]{:S(2)}, u32[]{:S(2)}) collective-permute-start(bf16[16,64,128]{2,1,0:T(8,128)(2,1)S(1)} %fusion.120), channel_id=1, source_target_pairs={{0,8},{8,16},{16,24},{24,32},{32,40},{40,48},{48,56},{56,64},{64,7... | collective-permute-start | bytes 786440 | tf_op jit(solution)/shard_map/while/body/eval_jaxpr/ppermute | solution.py:16
  86.4 8.3 %collective-permute-start = (bf16[16,64,128]{2,1,0:T(8,128)(2,1)S(1)}, bf16[16,64,128]{2,1,0:T(8,128)(2,1)S(1)}, u32[]{:S(2)}, u32[]{:S(2)}) collective-permute-start(bf16[16,64,128]{2,1,0:T(8,128)(2,1)S(1)} %fusion.120), channel_id=1, source_target_pairs={{0,8},{8,16},{16,24},{24,32},{32,40},{40,48},{48,56},{56,64},{64,7... | collective-permute-start | bytes 786440 | tf_op jit(solution)/shard_map/while/body/eval_jaxpr/ppermute | solution.py:16
  96.0 7.2 %collective-permute-start = (bf16[16,64,128]{2,1,0:T(8,128)(2,1)S(1)}, bf16[16,64,128]{2,1,0:T(8,128)(2,1)S(1)}, u32[]{:S(2)}, u32[]{:S(2)}) collective-permute-start(bf16[16,64,128]{2,1,0:T(8,128)(2,1)S(1)} %fusion.120), channel_id=1, source_target_pairs={{0,8},{8,16},{16,24},{24,32},{32,40},{40,48},{48,56},{56,64},{64,7... | collective-permute-start | bytes 786440 | tf_op jit(solution)/shard_map/while/body/eval_jaxpr/ppermute | solution.py:16
  104.6 12.2 %collective-permute-start = (bf16[16,64,128]{2,1,0:T(8,128)(2,1)S(1)}, bf16[16,64,128]{2,1,0:T(8,128)(2,1)S(1)}, u32[]{:S(2)}, u32[]{:S(2)}) collective-permute-start(bf16[16,64,128]{2,1,0:T(8,128)(2,1)S(1)} %fusion.120), channel_id=1, source_target_pairs={{0,8},{8,16},{16,24},{24,32},{32,40},{40,48},{48,56},{56,64},{64,7... | collective-permute-start | bytes 786440 | tf_op jit(solution)/shard_map/while/body/eval_jaxpr/ppermute | solution.py:16
  118.1 11.3 %collective-permute-start = (bf16[16,64,128]{2,1,0:T(8,128)(2,1)S(1)}, bf16[16,64,128]{2,1,0:T(8,128)(2,1)S(1)}, u32[]{:S(2)}, u32[]{:S(2)}) collective-permute-start(bf16[16,64,128]{2,1,0:T(8,128)(2,1)S(1)} %fusion.120), channel_id=1, source_target_pairs={{0,8},{8,16},{16,24},{24,32},{32,40},{40,48},{48,56},{56,64},{64,7... | collective-permute-start | bytes 786440 | tf_op jit(solution)/shard_map/while/body/eval_jaxpr/ppermute | solution.py:16
  130.7 14.2 %collective-permute-start = (bf16[16,64,128]{2,1,0:T(8,128)(2,1)S(1)}, bf16[16,64,128]{2,1,0:T(8,128)(2,1)S(1)}, u32[]{:S(2)}, u32[]{:S(2)}) collective-permute-start(bf16[16,64,128]{2,1,0:T(8,128)(2,1)S(1)} %fusion.120), channel_id=1, source_target_pairs={{0,8},{8,16},{16,24},{24,32},{32,40},{40,48},{48,56},{56,64},{64,7... | collective-permute-start | bytes 786440 | tf_op jit(solution)/shard_map/while/body/eval_jaxpr/ppermute | solution.py:16
  146.2 9.3 %collective-permute-start = (bf16[16,64,128]{2,1,0:T(8,128)(2,1)S(1)}, bf16[16,64,128]{2,1,0:T(8,128)(2,1)S(1)}, u32[]{:S(2)}, u32[]{:S(2)}) collective-permute-start(bf16[16,64,128]{2,1,0:T(8,128)(2,1)S(1)} %fusion.120), channel_id=1, source_target_pairs={{0,8},{8,16},{16,24},{24,32},{32,40},{40,48},{48,56},{56,64},{64,7... | collective-permute-start | bytes 786440 | tf_op jit(solution)/shard_map/while/body/eval_jaxpr/ppermute | solution.py:16
  165.3 7.9 %multiply_reduce_fusion.2 = (f32[256]{0:T(256)S(1)}, f32[256]{0:T(256)S(1)}, f32[256,1024]{1,0:T(8,128)}) fusion(f32[256,1024]{1,0:T(8,128)S(1)} %copy.52, bf16[256,1024]{1,0:T(8,128)(2,1)} %param.16, f32[1024]{0:T(1024)} %param.19, bf16[256,4096]{1,0:T(8,128)(2,1)} %all-gather.5.cloned.1.call-done, bf16[4096,1024]{1,0:T(8,128)(2,1)} %all-gather.3.cloned.1.call-done), kind=kOutput, calls=%fused_computation.78 | convolution fusion | flops 2150366720 | bytes 13113344 | tf_op jit(solution)/shard_map/dot_general | solution.py:135
  186.8 193.5 %while.7 = (s32[]{:T(128)}, f32[16,64,128]{2,1,0:T(8,128)S(1)}, f32[16]{0:T(128)}, f32[16,64,128]{2,1,0:T(8,128)S(1)}, s32[]{:T(128)}, /*index=5*/s32[]{:T(128)}) while((s32[]{:T(128)}, f32[16,64,128]{2,1,0:T(8,128)S(1)}, f32[16]{0:T(128)}, f32[16,64,128]{2,1,0:T(8,128)S(1)}, s32[]{:T(128)}, /*index=5*/s32[]{:T(128)}) %tuple.86), condition=%wide.region_12.13_spmd.clone, body=%wide.region_11.12_spmd.clone.sunk | while | flops 655363 | bytes 3145911 | solution.py:151
  189.0 9.0 %collective-permute-done.1 = bf16[16,64,128]{2,1,0:T(8,128)(2,1)S(1)} collective-permute-done((bf16[16,64,128]{2,1,0:T(8,128)(2,1)S(1)}, bf16[16,64,128]{2,1,0:T(8,128)(2,1)S(1)}, u32[]{:S(2)}, u32[]{:S(2)}) %collective-permute-start.1) | collective-permute-done | bytes 262176 | tf_op jit(solution)/shard_map/while/body/eval_jaxpr/ppermute | solution.py:16
  200.1 9.9 %collective-permute-done.1 = bf16[16,64,128]{2,1,0:T(8,128)(2,1)S(1)} collective-permute-done((bf16[16,64,128]{2,1,0:T(8,128)(2,1)S(1)}, bf16[16,64,128]{2,1,0:T(8,128)(2,1)S(1)}, u32[]{:S(2)}, u32[]{:S(2)}) %collective-permute-start.1) | collective-permute-done | bytes 262176 | tf_op jit(solution)/shard_map/while/body/eval_jaxpr/ppermute | solution.py:16
  212.1 9.8 %collective-permute-done.1 = bf16[16,64,128]{2,1,0:T(8,128)(2,1)S(1)} collective-permute-done((bf16[16,64,128]{2,1,0:T(8,128)(2,1)S(1)}, bf16[16,64,128]{2,1,0:T(8,128)(2,1)S(1)}, u32[]{:S(2)}, u32[]{:S(2)}) %collective-permute-start.1) | collective-permute-done | bytes 262176 | tf_op jit(solution)/shard_map/while/body/eval_jaxpr/ppermute | solution.py:16
  224.0 10.8 %collective-permute-done.1 = bf16[16,64,128]{2,1,0:T(8,128)(2,1)S(1)} collective-permute-done((bf16[16,64,128]{2,1,0:T(8,128)(2,1)S(1)}, bf16[16,64,128]{2,1,0:T(8,128)(2,1)S(1)}, u32[]{:S(2)}, u32[]{:S(2)}) %collective-permute-start.1) | collective-permute-done | bytes 262176 | tf_op jit(solution)/shard_map/while/body/eval_jaxpr/ppermute | solution.py:16
  236.9 10.0 %collective-permute-done.1 = bf16[16,64,128]{2,1,0:T(8,128)(2,1)S(1)} collective-permute-done((bf16[16,64,128]{2,1,0:T(8,128)(2,1)S(1)}, bf16[16,64,128]{2,1,0:T(8,128)(2,1)S(1)}, u32[]{:S(2)}, u32[]{:S(2)}) %collective-permute-start.1) | collective-permute-done | bytes 262176 | tf_op jit(solution)/shard_map/while/body/eval_jaxpr/ppermute | solution.py:16
  249.0 11.1 %collective-permute-done.1 = bf16[16,64,128]{2,1,0:T(8,128)(2,1)S(1)} collective-permute-done((bf16[16,64,128]{2,1,0:T(8,128)(2,1)S(1)}, bf16[16,64,128]{2,1,0:T(8,128)(2,1)S(1)}, u32[]{:S(2)}, u32[]{:S(2)}) %collective-permute-start.1) | collective-permute-done | bytes 262176 | tf_op jit(solution)/shard_map/while/body/eval_jaxpr/ppermute | solution.py:16
  262.2 15.5 %collective-permute-done.1 = bf16[16,64,128]{2,1,0:T(8,128)(2,1)S(1)} collective-permute-done((bf16[16,64,128]{2,1,0:T(8,128)(2,1)S(1)}, bf16[16,64,128]{2,1,0:T(8,128)(2,1)S(1)}, u32[]{:S(2)}, u32[]{:S(2)}) %collective-permute-start.1) | collective-permute-done | bytes 262176 | tf_op jit(solution)/shard_map/while/body/eval_jaxpr/ppermute | solution.py:16
  279.9 14.2 %collective-permute-done.1 = bf16[16,64,128]{2,1,0:T(8,128)(2,1)S(1)} collective-permute-done((bf16[16,64,128]{2,1,0:T(8,128)(2,1)S(1)}, bf16[16,64,128]{2,1,0:T(8,128)(2,1)S(1)}, u32[]{:S(2)}, u32[]{:S(2)}) %collective-permute-start.1) | collective-permute-done | bytes 262176 | tf_op jit(solution)/shard_map/while/body/eval_jaxpr/ppermute | solution.py:16
  296.2 9.5 %collective-permute-done.1 = bf16[16,64,128]{2,1,0:T(8,128)(2,1)S(1)} collective-permute-done((bf16[16,64,128]{2,1,0:T(8,128)(2,1)S(1)}, bf16[16,64,128]{2,1,0:T(8,128)(2,1)S(1)}, u32[]{:S(2)}, u32[]{:S(2)}) %collective-permute-start.1) | collective-permute-done | bytes 262176 | tf_op jit(solution)/shard_map/while/body/eval_jaxpr/ppermute | solution.py:16
  307.7 12.2 %collective-permute-done.1 = bf16[16,64,128]{2,1,0:T(8,128)(2,1)S(1)} collective-permute-done((bf16[16,64,128]{2,1,0:T(8,128)(2,1)S(1)}, bf16[16,64,128]{2,1,0:T(8,128)(2,1)S(1)}, u32[]{:S(2)}, u32[]{:S(2)}) %collective-permute-start.1) | collective-permute-done | bytes 262176 | tf_op jit(solution)/shard_map/while/body/eval_jaxpr/ppermute | solution.py:16
  322.0 8.5 %collective-permute-done.1 = bf16[16,64,128]{2,1,0:T(8,128)(2,1)S(1)} collective-permute-done((bf16[16,64,128]{2,1,0:T(8,128)(2,1)S(1)}, bf16[16,64,128]{2,1,0:T(8,128)(2,1)S(1)}, u32[]{:S(2)}, u32[]{:S(2)}) %collective-permute-start.1) | collective-permute-done | bytes 262176 | tf_op jit(solution)/shard_map/while/body/eval_jaxpr/ppermute | solution.py:16
  332.7 9.8 %collective-permute-done.1 = bf16[16,64,128]{2,1,0:T(8,128)(2,1)S(1)} collective-permute-done((bf16[16,64,128]{2,1,0:T(8,128)(2,1)S(1)}, bf16[16,64,128]{2,1,0:T(8,128)(2,1)S(1)}, u32[]{:S(2)}, u32[]{:S(2)}) %collective-permute-start.1) | collective-permute-done | bytes 262176 | tf_op jit(solution)/shard_map/while/body/eval_jaxpr/ppermute | solution.py:16
  344.6 10.0 %collective-permute-done.1 = bf16[16,64,128]{2,1,0:T(8,128)(2,1)S(1)} collective-permute-done((bf16[16,64,128]{2,1,0:T(8,128)(2,1)S(1)}, bf16[16,64,128]{2,1,0:T(8,128)(2,1)S(1)}, u32[]{:S(2)}, u32[]{:S(2)}) %collective-permute-start.1) | collective-permute-done | bytes 262176 | tf_op jit(solution)/shard_map/while/body/eval_jaxpr/ppermute | solution.py:16
  356.7 11.4 %collective-permute-done.1 = bf16[16,64,128]{2,1,0:T(8,128)(2,1)S(1)} collective-permute-done((bf16[16,64,128]{2,1,0:T(8,128)(2,1)S(1)}, bf16[16,64,128]{2,1,0:T(8,128)(2,1)S(1)}, u32[]{:S(2)}, u32[]{:S(2)}) %collective-permute-start.1) | collective-permute-done | bytes 262176 | tf_op jit(solution)/shard_map/while/body/eval_jaxpr/ppermute | solution.py:16
  370.2 10.0 %collective-permute-done.1 = bf16[16,64,128]{2,1,0:T(8,128)(2,1)S(1)} collective-permute-done((bf16[16,64,128]{2,1,0:T(8,128)(2,1)S(1)}, bf16[16,64,128]{2,1,0:T(8,128)(2,1)S(1)}, u32[]{:S(2)}, u32[]{:S(2)}) %collective-permute-start.1) | collective-permute-done | bytes 262176 | tf_op jit(solution)/shard_map/while/body/eval_jaxpr/ppermute | solution.py:16
  383.8 7.8 %convolution_convert_fusion = bf16[256,4096]{1,0:T(8,128)(2,1)} fusion(bf16[4096,1024]{1,0:T(8,128)(2,1)} %all-gather.3.cloned.1.call-done, f32[1024]{0:T(1024)S(1)} %copy-done.39, f32[256]{0:T(256)S(1)} %copy-done.35, f32[256,1024]{1,0:T(8,128)} %copy-done.5, bf16[256,1024]{1,0:T(8,128)(2,1)} %param.16), kind=kOutput, calls=%fused_computation.10 | convolution fusion | flops 2150891520 | bytes 12063744 | tf_op jit(solution)/shard_map/dot_general | solution.py:128
  403.6 7.3 %fusion.68 = (f32[16,256]{1,0:T(8,128)S(1)}, f32[16,256]{1,0:T(8,128)S(1)}, f32[256,256]{1,0:T(8,128)}) fusion(f32[16,256]{1,0:T(8,128)S(1)} %copy_bitcast_fusion, f32[256,256]{1,0:T(8,128)S(1)} %fusion.89, pred[256,256]{1,0:T(8,128)(4,1)S(1)} %compare_and_fusion, f32[256,16,64]{0,2,1:T(8,128)S(1)} %copy-done.2, f32[256,16,64]{0,2,1:T(8,128)S(1)} %bitcast.183), kind=kOutput, calls=%fused_computation.89 | convolution fusion | flops 820961280 | bytes 2736128 | tf_op jit(solution)/shard_map/transpose(jvp())/while/body/eval_jaxpr/checkpoint/hts,shp->thp/dot_general | solution.py:42
  440.1 49.1 %reduce-scatter.3.cloned.1.call-done = bf16[256,512]{1,0:T(8,128)(2,1)} async-done(((bf16[256,4096]{1,0:T(8,128)(2,1)}), bf16[256,512]{1,0:T(8,128)(2,1)}) %reduce-scatter.3.cloned.1.call-update) | async-done | bytes 262160 | tf_op jit(solution)/shard_map/reduce_scatter | solution.py:131
  (268 shorter events, 149.9 us)
Async XLA Ops:
  7.2 158.1 %all-gather.5.cloned.1.call-start = ((), (), s32[]{:S(2)}) async-start(), calls=%async_computation.4 | async-start | bytes 2359296 | tf_op jit(solution)/shard_map/all_gather | solution.py:134
  7.9 157.4 %all-gather.3.cloned.1.call-start = ((), (), s32[]{:S(2)}) async-start(), calls=%async_computation.2 | async-start | bytes 8912896 | tf_op jit(solution)/shard_map/all_gather | solution.py:127
  8.6 429.3 %reduce-scatter.5.cloned.1.call-start = ((), (), s32[]{:S(2)}) async-start(), calls=%async_computation.5 | async-start | bytes 8912896 | tf_op jit(solution)/shard_map/reduce_scatter | solution.py:136
  31.1 7.7 %collective-permute-start = (bf16[16,64,128]{2,1,0:T(8,128)(2,1)S(1)}, bf16[16,64,128]{2,1,0:T(8,128)(2,1)S(1)}, u32[]{:S(2)}, u32[]{:S(2)}) collective-permute-start(bf16[16,64,128]{2,1,0:T(8,128)(2,1)S(1)} %fusion.120), channel_id=1, source_target_pairs={{0,8},{8,16},{16,24},{24,32},{32,40},{40,48},{48,56},{56,64},{64,7... | collective-permute-start | bytes 786440 | tf_op jit(solution)/shard_map/while/body/eval_jaxpr/ppermute | solution.py:16
  39.0 7.7 %collective-permute-start = (bf16[16,64,128]{2,1,0:T(8,128)(2,1)S(1)}, bf16[16,64,128]{2,1,0:T(8,128)(2,1)S(1)}, u32[]{:S(2)}, u32[]{:S(2)}) collective-permute-start(bf16[16,64,128]{2,1,0:T(8,128)(2,1)S(1)} %fusion.120), channel_id=1, source_target_pairs={{0,8},{8,16},{16,24},{24,32},{32,40},{40,48},{48,56},{56,64},{64,7... | collective-permute-start | bytes 786440 | tf_op jit(solution)/shard_map/while/body/eval_jaxpr/ppermute | solution.py:16
  46.9 7.7 %collective-permute-start = (bf16[16,64,128]{2,1,0:T(8,128)(2,1)S(1)}, bf16[16,64,128]{2,1,0:T(8,128)(2,1)S(1)}, u32[]{:S(2)}, u32[]{:S(2)}) collective-permute-start(bf16[16,64,128]{2,1,0:T(8,128)(2,1)S(1)} %fusion.120), channel_id=1, source_target_pairs={{0,8},{8,16},{16,24},{24,32},{32,40},{40,48},{48,56},{56,64},{64,7... | collective-permute-start | bytes 786440 | tf_op jit(solution)/shard_map/while/body/eval_jaxpr/ppermute | solution.py:16
  54.8 7.7 %collective-permute-start = (bf16[16,64,128]{2,1,0:T(8,128)(2,1)S(1)}, bf16[16,64,128]{2,1,0:T(8,128)(2,1)S(1)}, u32[]{:S(2)}, u32[]{:S(2)}) collective-permute-start(bf16[16,64,128]{2,1,0:T(8,128)(2,1)S(1)} %fusion.120), channel_id=1, source_target_pairs={{0,8},{8,16},{16,24},{24,32},{32,40},{40,48},{48,56},{56,64},{64,7... | collective-permute-start | bytes 786440 | tf_op jit(solution)/shard_map/while/body/eval_jaxpr/ppermute | solution.py:16
  62.7 7.7 %collective-permute-start = (bf16[16,64,128]{2,1,0:T(8,128)(2,1)S(1)}, bf16[16,64,128]{2,1,0:T(8,128)(2,1)S(1)}, u32[]{:S(2)}, u32[]{:S(2)}) collective-permute-start(bf16[16,64,128]{2,1,0:T(8,128)(2,1)S(1)} %fusion.120), channel_id=1, source_target_pairs={{0,8},{8,16},{16,24},{24,32},{32,40},{40,48},{48,56},{56,64},{64,7... | collective-permute-start | bytes 786440 | tf_op jit(solution)/shard_map/while/body/eval_jaxpr/ppermute | solution.py:16
  70.6 7.7 %collective-permute-start = (bf16[16,64,128]{2,1,0:T(8,128)(2,1)S(1)}, bf16[16,64,128]{2,1,0:T(8,128)(2,1)S(1)}, u32[]{:S(2)}, u32[]{:S(2)}) collective-permute-start(bf16[16,64,128]{2,1,0:T(8,128)(2,1)S(1)} %fusion.120), channel_id=1, source_target_pairs={{0,8},{8,16},{16,24},{24,32},{32,40},{40,48},{48,56},{56,64},{64,7... | collective-permute-start | bytes 786440 | tf_op jit(solution)/shard_map/while/body/eval_jaxpr/ppermute | solution.py:16
  78.5 7.7 %collective-permute-start = (bf16[16,64,128]{2,1,0:T(8,128)(2,1)S(1)}, bf16[16,64,128]{2,1,0:T(8,128)(2,1)S(1)}, u32[]{:S(2)}, u32[]{:S(2)}) collective-permute-start(bf16[16,64,128]{2,1,0:T(8,128)(2,1)S(1)} %fusion.120), channel_id=1, source_target_pairs={{0,8},{8,16},{16,24},{24,32},{32,40},{40,48},{48,56},{56,64},{64,7... | collective-permute-start | bytes 786440 | tf_op jit(solution)/shard_map/while/body/eval_jaxpr/ppermute | solution.py:16
  86.4 9.4 %collective-permute-start = (bf16[16,64,128]{2,1,0:T(8,128)(2,1)S(1)}, bf16[16,64,128]{2,1,0:T(8,128)(2,1)S(1)}, u32[]{:S(2)}, u32[]{:S(2)}) collective-permute-start(bf16[16,64,128]{2,1,0:T(8,128)(2,1)S(1)} %fusion.120), channel_id=1, source_target_pairs={{0,8},{8,16},{16,24},{24,32},{32,40},{40,48},{48,56},{56,64},{64,7... | collective-permute-start | bytes 786440 | tf_op jit(solution)/shard_map/while/body/eval_jaxpr/ppermute | solution.py:16
  96.0 8.4 %collective-permute-start = (bf16[16,64,128]{2,1,0:T(8,128)(2,1)S(1)}, bf16[16,64,128]{2,1,0:T(8,128)(2,1)S(1)}, u32[]{:S(2)}, u32[]{:S(2)}) collective-permute-start(bf16[16,64,128]{2,1,0:T(8,128)(2,1)S(1)} %fusion.120), channel_id=1, source_target_pairs={{0,8},{8,16},{16,24},{24,32},{32,40},{40,48},{48,56},{56,64},{64,7... | collective-permute-start | bytes 786440 | tf_op jit(solution)/shard_map/while/body/eval_jaxpr/ppermute | solution.py:16
  104.6 13.3 %collective-permute-start = (bf16[16,64,128]{2,1,0:T(8,128)(2,1)S(1)}, bf16[16,64,128]{2,1,0:T(8,128)(2,1)S(1)}, u32[]{:S(2)}, u32[]{:S(2)}) collective-permute-start(bf16[16,64,128]{2,1,0:T(8,128)(2,1)S(1)} %fusion.120), channel_id=1, source_target_pairs={{0,8},{8,16},{16,24},{24,32},{32,40},{40,48},{48,56},{56,64},{64,7... | collective-permute-start | bytes 786440 | tf_op jit(solution)/shard_map/while/body/eval_jaxpr/ppermute | solution.py:16
  118.1 12.4 %collective-permute-start = (bf16[16,64,128]{2,1,0:T(8,128)(2,1)S(1)}, bf16[16,64,128]{2,1,0:T(8,128)(2,1)S(1)}, u32[]{:S(2)}, u32[]{:S(2)}) collective-permute-start(bf16[16,64,128]{2,1,0:T(8,128)(2,1)S(1)} %fusion.120), channel_id=1, source_target_pairs={{0,8},{8,16},{16,24},{24,32},{32,40},{40,48},{48,56},{56,64},{64,7... | collective-permute-start | bytes 786440 | tf_op jit(solution)/shard_map/while/body/eval_jaxpr/ppermute | solution.py:16
  130.7 15.3 %collective-permute-start = (bf16[16,64,128]{2,1,0:T(8,128)(2,1)S(1)}, bf16[16,64,128]{2,1,0:T(8,128)(2,1)S(1)}, u32[]{:S(2)}, u32[]{:S(2)}) collective-permute-start(bf16[16,64,128]{2,1,0:T(8,128)(2,1)S(1)} %fusion.120), channel_id=1, source_target_pairs={{0,8},{8,16},{16,24},{24,32},{32,40},{40,48},{48,56},{56,64},{64,7... | collective-permute-start | bytes 786440 | tf_op jit(solution)/shard_map/while/body/eval_jaxpr/ppermute | solution.py:16
  146.2 10.4 %collective-permute-start = (bf16[16,64,128]{2,1,0:T(8,128)(2,1)S(1)}, bf16[16,64,128]{2,1,0:T(8,128)(2,1)S(1)}, u32[]{:S(2)}, u32[]{:S(2)}) collective-permute-start(bf16[16,64,128]{2,1,0:T(8,128)(2,1)S(1)} %fusion.120), channel_id=1, source_target_pairs={{0,8},{8,16},{16,24},{24,32},{32,40},{40,48},{48,56},{56,64},{64,7... | collective-permute-start | bytes 786440 | tf_op jit(solution)/shard_map/while/body/eval_jaxpr/ppermute | solution.py:16
  179.7 309.5 %reduce-scatter.3.cloned.1.call-start = ((), (), s32[]{:S(2)}) async-start(), calls=%async_computation.3 | async-start | bytes 2359296 | tf_op jit(solution)/shard_map/reduce_scatter | solution.py:131
  187.7 10.3 %collective-permute-start.1 = (bf16[16,64,128]{2,1,0:T(8,128)(2,1)S(1)}, bf16[16,64,128]{2,1,0:T(8,128)(2,1)S(1)}, u32[]{:S(2)}, u32[]{:S(2)}) collective-permute-start(bf16[16,64,128]{2,1,0:T(8,128)(2,1)S(1)} %fusion.121), channel_id=1, source_target_pairs={{8,0},{16,8},{24,16},{32,24},{40,32},{48,40},{56,48},{64,56},{72,6... | collective-permute-start | bytes 786440 | tf_op jit(solution)/shard_map/while/body/eval_jaxpr/ppermute | solution.py:16
  198.8 11.2 %collective-permute-start.1 = (bf16[16,64,128]{2,1,0:T(8,128)(2,1)S(1)}, bf16[16,64,128]{2,1,0:T(8,128)(2,1)S(1)}, u32[]{:S(2)}, u32[]{:S(2)}) collective-permute-start(bf16[16,64,128]{2,1,0:T(8,128)(2,1)S(1)} %fusion.121), channel_id=1, source_target_pairs={{8,0},{16,8},{24,16},{32,24},{40,32},{48,40},{56,48},{64,56},{72,6... | collective-permute-start | bytes 786440 | tf_op jit(solution)/shard_map/while/body/eval_jaxpr/ppermute | solution.py:16
  210.8 11.1 %collective-permute-start.1 = (bf16[16,64,128]{2,1,0:T(8,128)(2,1)S(1)}, bf16[16,64,128]{2,1,0:T(8,128)(2,1)S(1)}, u32[]{:S(2)}, u32[]{:S(2)}) collective-permute-start(bf16[16,64,128]{2,1,0:T(8,128)(2,1)S(1)} %fusion.121), channel_id=1, source_target_pairs={{8,0},{16,8},{24,16},{32,24},{40,32},{48,40},{56,48},{64,56},{72,6... | collective-permute-start | bytes 786440 | tf_op jit(solution)/shard_map/while/body/eval_jaxpr/ppermute | solution.py:16
  222.7 12.1 %collective-permute-start.1 = (bf16[16,64,128]{2,1,0:T(8,128)(2,1)S(1)}, bf16[16,64,128]{2,1,0:T(8,128)(2,1)S(1)}, u32[]{:S(2)}, u32[]{:S(2)}) collective-permute-start(bf16[16,64,128]{2,1,0:T(8,128)(2,1)S(1)} %fusion.121), channel_id=1, source_target_pairs={{8,0},{16,8},{24,16},{32,24},{40,32},{48,40},{56,48},{64,56},{72,6... | collective-permute-start | bytes 786440 | tf_op jit(solution)/shard_map/while/body/eval_jaxpr/ppermute | solution.py:16
  235.6 11.3 %collective-permute-start.1 = (bf16[16,64,128]{2,1,0:T(8,128)(2,1)S(1)}, bf16[16,64,128]{2,1,0:T(8,128)(2,1)S(1)}, u32[]{:S(2)}, u32[]{:S(2)}) collective-permute-start(bf16[16,64,128]{2,1,0:T(8,128)(2,1)S(1)} %fusion.121), channel_id=1, source_target_pairs={{8,0},{16,8},{24,16},{32,24},{40,32},{48,40},{56,48},{64,56},{72,6... | collective-permute-start | bytes 786440 | tf_op jit(solution)/shard_map/while/body/eval_jaxpr/ppermute | solution.py:16
  247.7 12.4 %collective-permute-start.1 = (bf16[16,64,128]{2,1,0:T(8,128)(2,1)S(1)}, bf16[16,64,128]{2,1,0:T(8,128)(2,1)S(1)}, u32[]{:S(2)}, u32[]{:S(2)}) collective-permute-start(bf16[16,64,128]{2,1,0:T(8,128)(2,1)S(1)} %fusion.121), channel_id=1, source_target_pairs={{8,0},{16,8},{24,16},{32,24},{40,32},{48,40},{56,48},{64,56},{72,6... | collective-permute-start | bytes 786440 | tf_op jit(solution)/shard_map/while/body/eval_jaxpr/ppermute | solution.py:16
  260.9 16.8 %collective-permute-start.1 = (bf16[16,64,128]{2,1,0:T(8,128)(2,1)S(1)}, bf16[16,64,128]{2,1,0:T(8,128)(2,1)S(1)}, u32[]{:S(2)}, u32[]{:S(2)}) collective-permute-start(bf16[16,64,128]{2,1,0:T(8,128)(2,1)S(1)} %fusion.121), channel_id=1, source_target_pairs={{8,0},{16,8},{24,16},{32,24},{40,32},{48,40},{56,48},{64,56},{72,6... | collective-permute-start | bytes 786440 | tf_op jit(solution)/shard_map/while/body/eval_jaxpr/ppermute | solution.py:16
  278.6 15.5 %collective-permute-start.1 = (bf16[16,64,128]{2,1,0:T(8,128)(2,1)S(1)}, bf16[16,64,128]{2,1,0:T(8,128)(2,1)S(1)}, u32[]{:S(2)}, u32[]{:S(2)}) collective-permute-start(bf16[16,64,128]{2,1,0:T(8,128)(2,1)S(1)} %fusion.121), channel_id=1, source_target_pairs={{8,0},{16,8},{24,16},{32,24},{40,32},{48,40},{56,48},{64,56},{72,6... | collective-permute-start | bytes 786440 | tf_op jit(solution)/shard_map/while/body/eval_jaxpr/ppermute | solution.py:16
  294.9 10.8 %collective-permute-start.1 = (bf16[16,64,128]{2,1,0:T(8,128)(2,1)S(1)}, bf16[16,64,128]{2,1,0:T(8,128)(2,1)S(1)}, u32[]{:S(2)}, u32[]{:S(2)}) collective-permute-start(bf16[16,64,128]{2,1,0:T(8,128)(2,1)S(1)} %fusion.121), channel_id=1, source_target_pairs={{8,0},{16,8},{24,16},{32,24},{40,32},{48,40},{56,48},{64,56},{72,6... | collective-permute-start | bytes 786440 | tf_op jit(solution)/shard_map/while/body/eval_jaxpr/ppermute | solution.py:16
  306.4 13.5 %collective-permute-start.1 = (bf16[16,64,128]{2,1,0:T(8,128)(2,1)S(1)}, bf16[16,64,128]{2,1,0:T(8,128)(2,1)S(1)}, u32[]{:S(2)}, u32[]{:S(2)}) collective-permute-start(bf16[16,64,128]{2,1,0:T(8,128)(2,1)S(1)} %fusion.121), channel_id=1, source_target_pairs={{8,0},{16,8},{24,16},{32,24},{40,32},{48,40},{56,48},{64,56},{72,6... | collective-permute-start | bytes 786440 | tf_op jit(solution)/shard_map/while/body/eval_jaxpr/ppermute | solution.py:16
  320.7 9.8 %collective-permute-start.1 = (bf16[16,64,128]{2,1,0:T(8,128)(2,1)S(1)}, bf16[16,64,128]{2,1,0:T(8,128)(2,1)S(1)}, u32[]{:S(2)}, u32[]{:S(2)}) collective-permute-start(bf16[16,64,128]{2,1,0:T(8,128)(2,1)S(1)} %fusion.121), channel_id=1, source_target_pairs={{8,0},{16,8},{24,16},{32,24},{40,32},{48,40},{56,48},{64,56},{72,6... | collective-permute-start | bytes 786440 | tf_op jit(solution)/shard_map/while/body/eval_jaxpr/ppermute | solution.py:16
  331.4 11.1 %collective-permute-start.1 = (bf16[16,64,128]{2,1,0:T(8,128)(2,1)S(1)}, bf16[16,64,128]{2,1,0:T(8,128)(2,1)S(1)}, u32[]{:S(2)}, u32[]{:S(2)}) collective-permute-start(bf16[16,64,128]{2,1,0:T(8,128)(2,1)S(1)} %fusion.121), channel_id=1, source_target_pairs={{8,0},{16,8},{24,16},{32,24},{40,32},{48,40},{56,48},{64,56},{72,6... | collective-permute-start | bytes 786440 | tf_op jit(solution)/shard_map/while/body/eval_jaxpr/ppermute | solution.py:16
  343.3 11.3 %collective-permute-start.1 = (bf16[16,64,128]{2,1,0:T(8,128)(2,1)S(1)}, bf16[16,64,128]{2,1,0:T(8,128)(2,1)S(1)}, u32[]{:S(2)}, u32[]{:S(2)}) collective-permute-start(bf16[16,64,128]{2,1,0:T(8,128)(2,1)S(1)} %fusion.121), channel_id=1, source_target_pairs={{8,0},{16,8},{24,16},{32,24},{40,32},{48,40},{56,48},{64,56},{72,6... | collective-permute-start | bytes 786440 | tf_op jit(solution)/shard_map/while/body/eval_jaxpr/ppermute | solution.py:16
  355.4 12.7 %collective-permute-start.1 = (bf16[16,64,128]{2,1,0:T(8,128)(2,1)S(1)}, bf16[16,64,128]{2,1,0:T(8,128)(2,1)S(1)}, u32[]{:S(2)}, u32[]{:S(2)}) collective-permute-start(bf16[16,64,128]{2,1,0:T(8,128)(2,1)S(1)} %fusion.121), channel_id=1, source_target_pairs={{8,0},{16,8},{24,16},{32,24},{40,32},{48,40},{56,48},{64,56},{72,6... | collective-permute-start | bytes 786440 | tf_op jit(solution)/shard_map/while/body/eval_jaxpr/ppermute | solution.py:16
  368.9 11.3 %collective-permute-start.1 = (bf16[16,64,128]{2,1,0:T(8,128)(2,1)S(1)}, bf16[16,64,128]{2,1,0:T(8,128)(2,1)S(1)}, u32[]{:S(2)}, u32[]{:S(2)}) collective-permute-start(bf16[16,64,128]{2,1,0:T(8,128)(2,1)S(1)} %fusion.121), channel_id=1, source_target_pairs={{8,0},{16,8},{24,16},{32,24},{40,32},{48,40},{56,48},{64,56},{72,6... | collective-permute-start | bytes 786440 | tf_op jit(solution)/shard_map/while/body/eval_jaxpr/ppermute | solution.py:16
  (42 other events, 1085.1 us)
Sparse Core Ops, SparseCore 0:
  9.6 66.0 all-gather.4
  78.2 70.4 all-gather.2
  179.8 155.2 reduce-scatter.4
  391.7 97.4 reduce-scatter.2
where the time goes:
time: 501 us; the launch traced here: 496 us
  waiting for transfers between devices  229 us (46%)
  starting transfers between devices  136 us (27%)
  matrix products  63.2 us (13%)
  other arithmetic  37.3 us (7%)
  between operations  15.2 us (3%)
  local copies, waits for them, and re-layouts  13.7 us (3%)
    ppermute x30, waiting for transfers between devices, from_behind(): lax.ppermute(value, axis, [(source, source + steps) for source in range(l...  179 us
    ppermute x30, starting transfers between devices, from_behind(): lax.ppermute(value, axis, [(source, source + steps) for source in range(l...  135 us
    reduce_scatter x1, waiting for transfers between devices, per_device(): lax.psum_scatter(partial_value.astype(jnp.bfloat16), 'head', scatter_dime...  49.1 us
    dot_general x3, matrix products, advance(): jnp.einsum('hts,shp->thp', scores, x_here, precision=lax.Precision.HIGHEST)  15.9 us
    convert_element_type x15, other arithmetic, backward_step(): (g_local[:, None, None] * carried + adjoint_in).astype(jnp.bfloat16)  10.9 us
  transfers between devices with their start and end apart: 34, of which 31 were waited for; matrix products, arithmetic and copies ran while one was open for 20% of the time, Pallas kernels for 0%

commit v1 on v0

--- a/solution.py
+++ b/solution.py
@@ -14,6 +14,35 @@
     count = lax.axis_size(axis)
     leading, last = (max(0, -steps), min(count, count - steps))
     return lax.ppermute(value, axis, [(source, source + steps) for source in range(leading, last)])
+
+
+def prefix_combine(decay, value, direction):
+    count = lax.axis_size("seq")
+
+    def shifted(item, steps):
+        return from_behind(item, "seq", direction * steps)
+
+    def sent(item):
+        return item.astype(jnp.bfloat16)
+
+    near = shifted(sent(value), 1).astype(jnp.float32)
+    total = near
+    window_decay = shifted(decay, 1)
+    window = 1
+    if count > 2:
+        far = shifted(sent(value), 2).astype(jnp.float32)
+        total = near + window_decay[:, None, None] * far
+        window_decay = window_decay * shifted(decay, 2)
+        window = 2
+    while window < count - 1:
+        incoming = shifted(sent(total), window).astype(jnp.float32)
+        next_decay = None
+        if 2 * window < count - 1:
+            next_decay = window_decay * shifted(window_decay, window)
+        total = total + window_decay[:, None, None] * incoming
+        window_decay = next_decay
+        window *= 2
+    return total
 
 
 def span_scan(inputs_x, inputs_b, inputs_c, log_decay, resets, start_state):
@@ -110,12 +139,7 @@
 
     g_local, pull_decay = jax.vjp(whole_decay, log_decay)
 
-    def forward_step(turn, carried):
-        return from_behind(
-            (g_local[:, None, None] * carried + s_local).astype(jnp.bfloat16), "seq", 1
-        ).astype(jnp.float32)
-
-    state_in = lax.fori_loop(0, lax.axis_size("seq") - 1, forward_step, zero_state)
+    state_in = prefix_combine(g_local, s_local, 1)
 
     def finish(y_arg, c_arg, decay_arg, z_arg, state_arg):
         return gated_norm(
@@ -143,12 +167,7 @@
     ).astype(jnp.float32)
     d_zero, d_c_two, d_decay_two, grad_z, adjoint_in = pull_finish(grad_y)
 
-    def backward_step(turn, carried):
-        return from_behind(
-            (g_local[:, None, None] * carried + adjoint_in).astype(jnp.bfloat16), "seq", -1
-        ).astype(jnp.float32)
-
-    adjoint_out = lax.fori_loop(0, lax.axis_size("seq") - 1, backward_step, zero_state)
+    adjoint_out = prefix_combine(g_local, adjoint_in, -1)
     grad_x, grad_b, d_c_one, d_decay_one = pull_scan((d_zero, adjoint_out))
     (d_decay_three,) = pull_decay(jnp.sum(adjoint_out * state_in, axis=(1, 2)))
     return (

time: 501 us -> 352 us (0.70)
  starting transfers between devices: 136 us -> 53.2 us
  waiting for transfers between devices: 229 us -> 172 us
  other arithmetic: 37.3 us -> 30.6 us
    ppermute x30 -> x18, waiting for transfers between devices: 179 us -> 53.1 us  [from_behind(): lax.ppermute(value, axis, [(source, source + steps) for source in range(l...]
    ppermute x30 -> x18, starting transfers between devices: 135 us -> 53.1 us  [from_behind(): lax.ppermute(value, axis, [(source, source + steps) for source in range(l...]
    all_gather x1, waiting for transfers between devices: 0.02 us -> 70.2 us  [per_device(): full_weight = lax.all_gather(out_weight, 'seq', axis=0, tiled=True)]
    reduce_scatter x1, waiting for transfers between devices: 49.1 us -> 37.9 us  [per_device(): lax.psum_scatter(partial_value.astype(jnp.bfloat16), 'head', scatter_dime...]
    convert_element_type x60 -> x6, other arithmetic: 14.1 us -> 3.34 us  [sent(): return item.astype(jnp.bfloat16)]
    all_gather x1, waiting for transfers between devices: 0.02 us -> 9.71 us  [per_device(): grad_full = lax.all_gather(out_grad, 'head', axis=1, tiled=True)]
  transfers between devices with their start and end apart: 34 -> 22, of which waited for: 31 -> 15; matrix products, arithmetic and copies ran while one was open for 20% -> 26% of each run, Pallas kernels for 0% -> 0%
where the time goes in v1:
time: 352 us; the launch traced here: 345 us
  waiting for transfers between devices  172 us (49%)
  matrix products  61 us (17%)
  starting transfers between devices  53.2 us (15%)
  other arithmetic  30.6 us (9%)
  between operations  15.5 us (4%)
  local copies, waits for them, and re-layouts  12.7 us (4%)
    all_gather x1, waiting for transfers between devices, per_device(): full_weight = lax.all_gather(out_weight, 'seq', axis=0, tiled=True)  70.2 us
    ppermute x18, waiting for transfers between devices, from_behind(): lax.ppermute(value, axis, [(source, source + steps) for source in range(l...  53.1 us
    ppermute x18, starting transfers between devices, from_behind(): lax.ppermute(value, axis, [(source, source + steps) for source in range(l...  53.1 us
    reduce_scatter x1, waiting for transfers between devices, per_device(): lax.psum_scatter(partial_value.astype(jnp.bfloat16), 'head', scatter_dime...  37.9 us
    dot_general x3, matrix products, advance(): jnp.einsum('hts,shp->thp', scores, x_here, precision=lax.Precision.HIGHEST)  15.1 us
    all_gather x1, waiting for transfers between devices, per_device(): grad_full = lax.all_gather(out_grad, 'head', axis=1, tiled=True)  9.71 us
    another operation x15, other arithmetic  9.46 us
    dot_general x3, matrix products, advance(): jnp.einsum('shp,shn->hpn', x_here * tail.T[:, :, None], b_heads, precisio...  8.14 us
  transfers between devices with their start and end apart: 22, of which 15 were waited for; matrix products, arithmetic and copies ran while one was open for 26% of the time, Pallas kernels for 0%

profile of v1, /device:TPU:0, one launch (start us, length us, event | category | flops | bytes accessed | tf_op | source)
XLA Modules:
  0.0 345.4 jit_solution(17509364376725708725)
XLA Ops:
  17.2 3.5 %collective-permute-start.2 = (bf16[16,64,128]{2,1,0:T(8,128)(2,1)S(1)}, bf16[16,64,128]{2,1,0:T(8,128)(2,1)S(1)}, u32[]{:S(2)}, u32[]{:S(2)}) collective-permute-start(bf16[16,64,128]{2,1,0:T(8,128)(2,1)S(1)} %fusion.38), channel_id=1, source_target_pairs={{0,16},{8,24},{16,32},{24,40},{32,48},{40,56},{48,64},{56,72},{64,... | collective-permute-start | bytes 786440 | tf_op jit(solution)/shard_map/ppermute | solution.py:16
  25.0 3.9 %collective-permute-start.1 = (f32[16]{0:T(128)S(1)}, f32[16]{0:T(128)S(1)}, u32[]{:S(2)}, u32[]{:S(2)}) collective-permute-start(f32[16]{0:T(128)S(1)} %exponential_multiply_fusion.1), channel_id=1, source_target_pairs={{0,8},{8,16},{16,24},{24,32},{32,40},{40,48},{48,56},{56,64},{64,7... | collective-permute-start | bytes 200 | tf_op jit(solution)/shard_map/ppermute | solution.py:16
  29.9 4.0 %collective-permute-start.4 = (bf16[16,64,128]{2,1,0:T(8,128)(2,1)S(1)}, bf16[16,64,128]{2,1,0:T(8,128)(2,1)S(1)}, u32[]{:S(2)}, u32[]{:S(2)}) collective-permute-start(bf16[16,64,128]{2,1,0:T(8,128)(2,1)S(1)} %fusion.72), channel_id=1, source_target_pairs={{0,16},{8,24},{16,32},{24,40},{32,48},{40,56},{48,64},{56,72},{64,... | collective-permute-start | bytes 786440 | tf_op jit(solution)/shard_map/ppermute | solution.py:16
  33.9 4.1 %collective-permute-start.3 = (f32[16]{0:T(128)S(1)}, f32[16]{0:T(128)S(1)}, u32[]{:S(2)}, u32[]{:S(2)}) collective-permute-start(f32[16]{0:T(128)S(1)} %exponential_multiply_fusion.1), channel_id=1, source_target_pairs={{0,16},{8,24},{16,32},{24,40},{32,48},{40,56},{48,64},{56,72},{64,... | collective-permute-start | bytes 200 | tf_op jit(solution)/shard_map/ppermute | solution.py:16
  39.6 9.1 %collective-permute-start.6 = (bf16[16,64,128]{2,1,0:T(8,128)(2,1)S(1)}, bf16[16,64,128]{2,1,0:T(8,128)(2,1)S(1)}, u32[]{:S(2)}, u32[]{:S(2)}) collective-permute-start(bf16[16,64,128]{2,1,0:T(8,128)(2,1)S(1)} %fusion.97), channel_id=1, source_target_pairs={{0,32},{8,40},{16,48},{24,56},{32,64},{40,72},{48,80},{56,88},{64,... | collective-permute-start | bytes 786440 | tf_op jit(solution)/shard_map/ppermute | solution.py:16
  49.0 3.6 %collective-permute-start.5 = (f32[16]{0:T(128)S(1)}, f32[16]{0:T(128)S(1)}, u32[]{:S(2)}, u32[]{:S(2)}) collective-permute-start(f32[16]{0:T(128)S(1)} %mul.426), channel_id=1, source_target_pairs={{0,16},{8,24},{16,32},{24,40},{32,48},{40,56},{48,64},{56,72},{64,... | collective-permute-start | bytes 200 | tf_op jit(solution)/shard_map/ppermute | solution.py:16
  54.2 10.0 %collective-permute-start.8 = (bf16[16,64,128]{2,1,0:T(8,128)(2,1)S(1)}, bf16[16,64,128]{2,1,0:T(8,128)(2,1)S(1)}, u32[]{:S(2)}, u32[]{:S(2)}) collective-permute-start(bf16[16,64,128]{2,1,0:T(8,128)(2,1)S(1)} %fusion.75), channel_id=1, source_target_pairs={{0,64},{8,72},{16,80},{24,88},{32,96},{40,104},{48,112},{56,120},{... | collective-permute-start | bytes 786440 | tf_op jit(solution)/shard_map/ppermute | solution.py:16
  64.2 3.2 fusion.28
  70.0 4.2 %collective-permute-done.8 = bf16[16,64,128]{2,1,0:T(8,128)(2,1)S(1)} collective-permute-done((bf16[16,64,128]{2,1,0:T(8,128)(2,1)S(1)}, bf16[16,64,128]{2,1,0:T(8,128)(2,1)S(1)}, u32[]{:S(2)}, u32[]{:S(2)}) %collective-permute-start.8) | collective-permute-done | bytes 262176 | tf_op jit(solution)/shard_map/ppermute | solution.py:16
  80.2 9.7 %all-gather.5.cloned.1.call-done = bf16[256,4096]{1,0:T(8,128)(2,1)} async-done(((bf16[256,512]{1,0:T(8,128)(2,1)}), bf16[256,4096]{1,0:T(8,128)(2,1)}) %all-gather.5.cloned.1.call-update) | async-done | bytes 2097168 | tf_op jit(solution)/shard_map/all_gather | solution.py:158
  89.9 70.2 %all-gather.3.cloned.1.call-done = bf16[4096,1024]{1,0:T(8,128)(2,1)} async-done(((bf16[256,1024]{1,0:T(8,128)(2,1)}), bf16[4096,1024]{1,0:T(8,128)(2,1)}) %all-gather.3.cloned.1.call-update) | async-done | bytes 8388624 | tf_op jit(solution)/shard_map/all_gather | solution.py:151
  160.1 7.6 %multiply_reduce_fusion.2 = (f32[256]{0:T(256)S(1)}, f32[256]{0:T(256)S(1)}, f32[256,1024]{1,0:T(8,128)}) fusion(f32[256,1024]{1,0:T(8,128)S(1)} %copy.52, bf16[256,1024]{1,0:T(8,128)(2,1)} %param.12, f32[1024]{0:T(1024)S(1)} %copy-done.30, bf16[256,4096]{1,0:T(8,128)(2,1)} %all-gather.5.cloned.1.call-done, bf16[4096,1024]{1,0:T(8,128)(2,1)} %all-gather.3.cloned.1.call-done), kind=kOutput, calls=%fused_computation.72 | convolution fusion | flops 2150366720 | bytes 13113344 | tf_op jit(solution)/shard_map/dot_general | solution.py:159
  167.8 5.8 %convert_bitcast_fusion = bf16[4096,1024]{0,1:T(8,128)(2,1)} fusion(bf16[256,4096]{1,0:T(8,128)(2,1)S(1)} %copy-done.29, f32[1024]{0:T(1024)S(1)} %copy-done.30, f32[256]{0:T(256)S(1)} %get-tuple-element.144, f32[256,1024]{1,0:T(8,128)S(1)} %copy.52, bf16[256,1024]{1,0:T(8,128)(2,1)S(1)} %copy-done.11), kind=kOutput, calls=%fused_computation | convolution fusion | flops 2154037248 | bytes 12063744 | tf_op jit(solution)/shard_map/dot_general | solution.py:161
  173.7 3.1 fusion.44
  182.2 2.5 collective-permute-done.10
  184.7 3.9 %collective-permute-done.11 = bf16[16,64,128]{2,1,0:T(8,128)(2,1)S(1)} collective-permute-done((bf16[16,64,128]{2,1,0:T(8,128)(2,1)S(1)}, bf16[16,64,128]{2,1,0:T(8,128)(2,1)S(1)}, u32[]{:S(2)}, u32[]{:S(2)}) %collective-permute-start.11) | collective-permute-done | bytes 262176 | tf_op jit(solution)/shard_map/ppermute | solution.py:16
  191.4 7.6 %collective-permute-done.12 = f32[16]{0:T(128)S(1)} collective-permute-done((f32[16]{0:T(128)}, f32[16]{0:T(128)S(1)}, u32[]{:S(2)}, u32[]{:S(2)}) %collective-permute-start.12) | collective-permute-done | bytes 96 | tf_op jit(solution)/shard_map/ppermute | solution.py:16
  200.9 4.4 %collective-permute-done.14 = f32[16]{0:T(128)S(1)} collective-permute-done((f32[16]{0:T(128)S(1)}, f32[16]{0:T(128)S(1)}, u32[]{:S(2)}, u32[]{:S(2)}) %collective-permute-start.14) | collective-permute-done | bytes 96 | tf_op jit(solution)/shard_map/ppermute | solution.py:16
  207.8 7.1 %collective-permute-done.16 = f32[16]{0:T(128)S(1)} collective-permute-done((f32[16]{0:T(128)S(1)}, f32[16]{0:T(128)S(1)}, u32[]{:S(2)}, u32[]{:S(2)}) %collective-permute-start.16) | collective-permute-done | bytes 96 | tf_op jit(solution)/shard_map/ppermute | solution.py:16
  217.8 7.4 %convolution_convert_fusion = bf16[256,4096]{1,0:T(8,128)(2,1)} fusion(bf16[4096,1024]{1,0:T(8,128)(2,1)} %all-gather.3.cloned.1.call-done, f32[1024]{0:T(1024)} %param.15, f32[256]{0:T(256)S(1)} %copy-done.26, f32[256,1024]{1,0:T(8,128)S(1)} %copy-done.5, bf16[256,1024]{1,0:T(8,128)(2,1)S(1)} %copy-done.12), kind=kOutput, calls=%fused_computation.4 | convolution fusion | flops 2150891520 | bytes 12063744 | tf_op jit(solution)/shard_map/dot_general | solution.py:152
  225.3 10.4 %collective-permute-done.15 = bf16[16,64,128]{2,1,0:T(8,128)(2,1)} collective-permute-done((bf16[16,64,128]{2,1,0:T(8,128)(2,1)}, bf16[16,64,128]{2,1,0:T(8,128)(2,1)}, u32[]{:S(2)}, u32[]{:S(2)}) %collective-permute-start.15) | collective-permute-done | bytes 262176 | tf_op jit(solution)/shard_map/ppermute | solution.py:16
  239.5 2.5 reduce-window.77
  242.8 8.6 %collective-permute-done.17 = bf16[16,64,128]{2,1,0:T(8,128)(2,1)S(1)} collective-permute-done((bf16[16,64,128]{2,1,0:T(8,128)(2,1)S(1)}, bf16[16,64,128]{2,1,0:T(8,128)(2,1)S(1)}, u32[]{:S(2)}, u32[]{:S(2)}) %collective-permute-start.17) | collective-permute-done | bytes 262176 | tf_op jit(solution)/shard_map/ppermute | solution.py:16
  257.5 4.1 %multiply_reduce_fusion.1 = (f32[256,16]{0,1:T(8,128)S(1)}, f32[256,16,64]{0,2,1:T(8,128)}) fusion(f32[256,16,64]{0,2,1:T(8,128)S(1)} %squeeze.51, f32[16,64,128]{2,1,0:T(8,128)S(1)} %get-tuple-element.77, f32[256,128]{1,0:T(8,128)} %bitcast.194), kind=kOutput, calls=%fused_computation.68 | convolution fusion | flops 403173376 | bytes 2768896 | tf_op jit(solution)/shard_map/transpose(jvp())/while/body/eval_jaxpr/checkpoint/shp,shn->hpn/dot_general | solution.py:80
  266.5 7.3 %fusion.65 = (f32[16,256]{1,0:T(8,128)S(1)}, f32[16,256]{1,0:T(8,128)S(1)}, f32[256,256]{1,0:T(8,128)}) fusion(f32[16,256]{1,0:T(8,128)S(1)} %copy_bitcast_fusion, f32[256,256]{1,0:T(8,128)S(1)} %fusion.90, pred[256,256]{1,0:T(8,128)(4,1)S(1)} %compare_and_fusion, f32[256,16,64]{0,2,1:T(8,128)S(1)} %squeeze.51, f32[256,16,64]{0,2,1:T(8,128)S(1)} %bitcast.185), kind=kOutput, calls=%fused_computation.84 | convolution fusion | flops 820961280 | bytes 2736128 | tf_op jit(solution)/shard_map/transpose(jvp())/while/body/eval_jaxpr/checkpoint/hts,shp->thp/dot_general | solution.py:71
  275.1 4.6 %fusion.34 = f32[256,16,64]{0,2,1:T(8,128)} fusion(f32[16,256]{1,0:T(8,128)S(1)} %copy_bitcast_fusion, f32[256,256]{1,0:T(8,128)S(1)} %fusion.90, pred[256,256]{1,0:T(8,128)(4,1)S(1)} %compare_and_fusion, f32[256,16,64]{0,2,1:T(8,128)S(1)} %bitcast.186, f32[256,16,64]{0,2,1:T(8,128)S(1)} %copy-done.9, f32[256,16]{0,1:T(8,128)S(1)} %get-tuple-element.139), kind=kOutput, calls=%fused_computation.44 | convolution fusion | flops 810024960 | bytes 3506176 | tf_op jit(solution)/shard_map/transpose(jvp())/while/body/eval_jaxpr/checkpoint/hts,shp->thp/dot_general | solution.py:71
  279.7 2.6 copy.62
  282.3 2.7 reduce-window.75
  285.7 2.9 convolution_bitcast_fusion.6
  288.6 2.5 convolution_bitcast_fusion.5
  295.8 2.5 fusion.39
  300.5 37.9 %reduce-scatter.3.cloned.1.call-done = bf16[256,512]{1,0:T(8,128)(2,1)} async-done(((bf16[256,4096]{1,0:T(8,128)(2,1)}), bf16[256,512]{1,0:T(8,128)(2,1)}) %reduce-scatter.3.cloned.1.call-update) | async-done | bytes 262160 | tf_op jit(solution)/shard_map/reduce_scatter | solution.py:155
  (178 shorter events, 66.0 us)
Async XLA Ops:
  7.2 41.6 %copy-start.15 = (bf16[256,128]{1,0:T(8,128)(2,1)S(1)}, bf16[256,128]{1,0:T(8,128)(2,1)}, u32[]{:S(2)}) copy-start(bf16[256,128]{1,0:T(8,128)(2,1)} %param.10) | copy-start | bytes 196612
  7.2 82.7 %all-gather.5.cloned.1.call-start = ((), (), s32[]{:S(2)}) async-start(), calls=%async_computation.4 | async-start | bytes 2359296 | tf_op jit(solution)/shard_map/all_gather | solution.py:158
  7.9 152.2 %all-gather.3.cloned.1.call-start = ((), (), s32[]{:S(2)}) async-start(), calls=%async_computation.2 | async-start | bytes 8912896 | tf_op jit(solution)/shard_map/all_gather | solution.py:151
  8.7 289.6 %reduce-scatter.5.cloned.1.call-start = ((), (), s32[]{:S(2)}) async-start(), calls=%async_computation.5 | async-start | bytes 8912896 | tf_op jit(solution)/shard_map/reduce_scatter | solution.py:160
  10.0 57.4 %copy-start.22 = (f32[256]{0:T(256)}, f32[256]{0:T(256)S(1)}, u32[]{:S(2)}) copy-start(f32[256]{0:T(256)S(1)} %get-tuple-element.130) | copy-start | bytes 3076
  12.1 55.3 %copy-start.21 = (f32[16,2]{0,1:T(2,128)}, f32[16,2]{0,1:T(2,128)S(1)}, u32[]{:S(2)}) copy-start(f32[16,2]{0,1:T(2,128)S(1)} %slice.68) | copy-start | bytes 388
  13.3 54.1 %copy-start.7 = (bf16[256,1024]{0,1:T(8,128)(2,1)}, bf16[256,1024]{0,1:T(8,128)(2,1)S(1)}, u32[]{:S(2)}) copy-start(bf16[256,1024]{0,1:T(8,128)(2,1)S(1)} %copy.51) | copy-start | bytes 1572868
  14.4 162.8 %copy-start.13 = (f32[16,256]{1,0:T(8,128)}, f32[16,256]{1,0:T(8,128)S(1)}, u32[]{:S(2)}) copy-start(f32[16,256]{1,0:T(8,128)S(1)} %get-tuple-element.141) | copy-start | bytes 49156
  17.2 12.6 %collective-permute-start.2 = (bf16[16,64,128]{2,1,0:T(8,128)(2,1)S(1)}, bf16[16,64,128]{2,1,0:T(8,128)(2,1)S(1)}, u32[]{:S(2)}, u32[]{:S(2)}) collective-permute-start(bf16[16,64,128]{2,1,0:T(8,128)(2,1)S(1)} %fusion.38), channel_id=1, source_target_pairs={{0,16},{8,24},{16,32},{24,40},{32,48},{40,56},{48,64},{56,72},{64,... | collective-permute-start | bytes 786440 | tf_op jit(solution)/shard_map/ppermute | solution.py:16
  20.7 9.1 %collective-permute-start = (bf16[16,64,128]{2,1,0:T(8,128)(2,1)S(1)}, bf16[16,64,128]{2,1,0:T(8,128)(2,1)S(1)}, u32[]{:S(2)}, u32[]{:S(2)}) collective-permute-start(bf16[16,64,128]{2,1,0:T(8,128)(2,1)S(1)} %fusion.38), channel_id=1, source_target_pairs={{0,8},{8,16},{16,24},{24,32},{32,40},{40,48},{48,56},{56,64},{64,7... | collective-permute-start | bytes 786440 | tf_op jit(solution)/shard_map/ppermute | solution.py:16
  23.0 44.4 %copy-start.28 = (f32[16]{0:T(128)}, f32[16]{0:T(128)S(1)}, u32[]{:S(2)}) copy-start(f32[16]{0:T(128)S(1)} %reduce_sum.139) | copy-start | bytes 196
  25.0 42.4 %copy-start.31 = (f32[16]{0:T(128)}, f32[16]{0:T(128)S(1)}, u32[]{:S(2)}) copy-start(f32[16]{0:T(128)S(1)} %exponential_multiply_fusion.1) | copy-start | bytes 196
  25.0 4.7 %collective-permute-start.1 = (f32[16]{0:T(128)S(1)}, f32[16]{0:T(128)S(1)}, u32[]{:S(2)}, u32[]{:S(2)}) collective-permute-start(f32[16]{0:T(128)S(1)} %exponential_multiply_fusion.1), channel_id=1, source_target_pairs={{0,8},{8,16},{16,24},{24,32},{32,40},{40,48},{48,56},{56,64},{64,7... | collective-permute-start | bytes 200 | tf_op jit(solution)/shard_map/ppermute | solution.py:16
  29.9 9.4 %collective-permute-start.4 = (bf16[16,64,128]{2,1,0:T(8,128)(2,1)S(1)}, bf16[16,64,128]{2,1,0:T(8,128)(2,1)S(1)}, u32[]{:S(2)}, u32[]{:S(2)}) collective-permute-start(bf16[16,64,128]{2,1,0:T(8,128)(2,1)S(1)} %fusion.72), channel_id=1, source_target_pairs={{0,16},{8,24},{16,32},{24,40},{32,48},{40,56},{48,64},{56,72},{64,... | collective-permute-start | bytes 786440 | tf_op jit(solution)/shard_map/ppermute | solution.py:16
  33.9 5.4 %collective-permute-start.3 = (f32[16]{0:T(128)S(1)}, f32[16]{0:T(128)S(1)}, u32[]{:S(2)}, u32[]{:S(2)}) collective-permute-start(f32[16]{0:T(128)S(1)} %exponential_multiply_fusion.1), channel_id=1, source_target_pairs={{0,16},{8,24},{16,32},{24,40},{32,48},{40,56},{48,64},{56,72},{64,... | collective-permute-start | bytes 200 | tf_op jit(solution)/shard_map/ppermute | solution.py:16
  39.6 14.2 %collective-permute-start.6 = (bf16[16,64,128]{2,1,0:T(8,128)(2,1)S(1)}, bf16[16,64,128]{2,1,0:T(8,128)(2,1)S(1)}, u32[]{:S(2)}, u32[]{:S(2)}) collective-permute-start(bf16[16,64,128]{2,1,0:T(8,128)(2,1)S(1)} %fusion.97), channel_id=1, source_target_pairs={{0,32},{8,40},{16,48},{24,56},{32,64},{40,72},{48,80},{56,88},{64,... | collective-permute-start | bytes 786440 | tf_op jit(solution)/shard_map/ppermute | solution.py:16
  49.0 4.9 %collective-permute-start.5 = (f32[16]{0:T(128)S(1)}, f32[16]{0:T(128)S(1)}, u32[]{:S(2)}, u32[]{:S(2)}) collective-permute-start(f32[16]{0:T(128)S(1)} %mul.426), channel_id=1, source_target_pairs={{0,16},{8,24},{16,32},{24,40},{32,48},{40,56},{48,64},{56,72},{64,... | collective-permute-start | bytes 200 | tf_op jit(solution)/shard_map/ppermute | solution.py:16
  54.2 20.0 %collective-permute-start.8 = (bf16[16,64,128]{2,1,0:T(8,128)(2,1)S(1)}, bf16[16,64,128]{2,1,0:T(8,128)(2,1)S(1)}, u32[]{:S(2)}, u32[]{:S(2)}) collective-permute-start(bf16[16,64,128]{2,1,0:T(8,128)(2,1)S(1)} %fusion.75), channel_id=1, source_target_pairs={{0,64},{8,72},{16,80},{24,88},{32,96},{40,104},{48,112},{56,120},{... | collective-permute-start | bytes 786440 | tf_op jit(solution)/shard_map/ppermute | solution.py:16
  67.4 2.6 collective-permute-start.7
  70.0 90.1 %copy-start.30 = (f32[1024]{0:T(1024)S(1)}, f32[1024]{0:T(1024)}, u32[]{:S(2)}) copy-start(f32[1024]{0:T(1024)} %param.15) | copy-start | bytes 12292
  80.1 93.6 %copy-start.4 = (f32[256,1024]{1,0:T(8,128)}, f32[256,1024]{1,0:T(8,128)S(1)}, u32[]{:S(2)}) copy-start(f32[256,1024]{1,0:T(8,128)S(1)} %copy.52) | copy-start | bytes 3145732
  80.2 87.6 %copy-start.11 = (bf16[256,1024]{1,0:T(8,128)(2,1)S(1)}, bf16[256,1024]{1,0:T(8,128)(2,1)}, u32[]{:S(2)}) copy-start(bf16[256,1024]{1,0:T(8,128)(2,1)} %param.12) | copy-start | bytes 1572868
  173.6 164.7 %reduce-scatter.3.cloned.1.call-start = ((), (), s32[]{:S(2)}) async-start(), calls=%async_computation.3 | async-start | bytes 2359296 | tf_op jit(solution)/shard_map/reduce_scatter | solution.py:155
  178.3 10.3 %collective-permute-start.11 = (bf16[16,64,128]{2,1,0:T(8,128)(2,1)S(1)}, bf16[16,64,128]{2,1,0:T(8,128)(2,1)S(1)}, u32[]{:S(2)}, u32[]{:S(2)}) collective-permute-start(bf16[16,64,128]{2,1,0:T(8,128)(2,1)S(1)} %convolution_convert_fusion.1), channel_id=1, source_target_pairs={{16,0},{24,8},{32,16},{40,24},{48,32},{56,40},{64,48},{72,56},{80,... | collective-permute-start | bytes 786440 | tf_op jit(solution)/shard_map/ppermute | solution.py:16
  179.6 9.0 %collective-permute-start.9 = (bf16[16,64,128]{2,1,0:T(8,128)(2,1)S(1)}, bf16[16,64,128]{2,1,0:T(8,128)(2,1)S(1)}, u32[]{:S(2)}, u32[]{:S(2)}) collective-permute-start(bf16[16,64,128]{2,1,0:T(8,128)(2,1)S(1)} %convolution_convert_fusion.1), channel_id=1, source_target_pairs={{8,0},{16,8},{24,16},{32,24},{40,32},{48,40},{56,48},{64,56},{72,6... | collective-permute-start | bytes 786440 | tf_op jit(solution)/shard_map/ppermute | solution.py:16
  180.9 3.8 %collective-permute-start.10 = (f32[16]{0:T(128)}, f32[16]{0:T(128)S(1)}, u32[]{:S(2)}, u32[]{:S(2)}) collective-permute-start(f32[16]{0:T(128)} %copy-done.31), channel_id=1, source_target_pairs={{8,0},{16,8},{24,16},{32,24},{40,32},{48,40},{56,48},{64,56},{72,6... | collective-permute-start | bytes 200 | tf_op jit(solution)/shard_map/ppermute | solution.py:16
  188.8 26.6 %collective-permute-start.13 = (bf16[16,64,128]{2,1,0:T(8,128)(2,1)S(1)}, bf16[16,64,128]{2,1,0:T(8,128)(2,1)S(1)}, u32[]{:S(2)}, u32[]{:S(2)}) collective-permute-start(bf16[16,64,128]{2,1,0:T(8,128)(2,1)S(1)} %fusion.73), channel_id=1, source_target_pairs={{16,0},{24,8},{32,16},{40,24},{48,32},{56,40},{64,48},{72,56},{80,... | collective-permute-start | bytes 786440 | tf_op jit(solution)/shard_map/ppermute | solution.py:16
  190.1 8.9 %collective-permute-start.12 = (f32[16]{0:T(128)}, f32[16]{0:T(128)S(1)}, u32[]{:S(2)}, u32[]{:S(2)}) collective-permute-start(f32[16]{0:T(128)} %copy-done.31), channel_id=1, source_target_pairs={{16,0},{24,8},{32,16},{40,24},{48,32},{56,40},{64,48},{72,56},{80,... | collective-permute-start | bytes 200 | tf_op jit(solution)/shard_map/ppermute | solution.py:16
  199.0 6.4 %collective-permute-start.14 = (f32[16]{0:T(128)S(1)}, f32[16]{0:T(128)S(1)}, u32[]{:S(2)}, u32[]{:S(2)}) collective-permute-start(f32[16]{0:T(128)S(1)} %mul.454), channel_id=1, source_target_pairs={{16,0},{24,8},{32,16},{40,24},{48,32},{56,40},{64,48},{72,56},{80,... | collective-permute-start | bytes 200 | tf_op jit(solution)/shard_map/ppermute | solution.py:16
  205.4 9.5 %collective-permute-start.16 = (f32[16]{0:T(128)S(1)}, f32[16]{0:T(128)S(1)}, u32[]{:S(2)}, u32[]{:S(2)}) collective-permute-start(f32[16]{0:T(128)S(1)} %mul.457), channel_id=1, source_target_pairs={{32,0},{40,8},{48,16},{56,24},{64,32},{72,40},{80,48},{88,56},{96,... | collective-permute-start | bytes 200 | tf_op jit(solution)/shard_map/ppermute | solution.py:16
  216.4 19.4 %collective-permute-start.15 = (bf16[16,64,128]{2,1,0:T(8,128)(2,1)}, bf16[16,64,128]{2,1,0:T(8,128)(2,1)}, u32[]{:S(2)}, u32[]{:S(2)}) collective-permute-start(bf16[16,64,128]{2,1,0:T(8,128)(2,1)} %fusion.98), channel_id=1, source_target_pairs={{32,0},{40,8},{48,16},{56,24},{64,32},{72,40},{80,48},{88,56},{96,... | collective-permute-start | bytes 786440 | tf_op jit(solution)/shard_map/ppermute | solution.py:16
  237.3 14.1 %collective-permute-start.17 = (bf16[16,64,128]{2,1,0:T(8,128)(2,1)S(1)}, bf16[16,64,128]{2,1,0:T(8,128)(2,1)S(1)}, u32[]{:S(2)}, u32[]{:S(2)}) collective-permute-start(bf16[16,64,128]{2,1,0:T(8,128)(2,1)S(1)} %fusion.76), channel_id=1, source_target_pairs={{64,0},{72,8},{80,16},{88,24},{96,32},{104,40},{112,48},{120,56},{... | collective-permute-start | bytes 786440 | tf_op jit(solution)/shard_map/ppermute | solution.py:16
  (22 other events, 372.1 us)
Sparse Core Ops, SparseCore 0:
  9.6 80.1 all-gather.4
  92.3 67.7 all-gather.2
  173.8 110.0 reduce-scatter.4
  286.7 51.6 reduce-scatter.2
